TPU v7x, 32 devices: a whole 2x2x4 slice. The times are simulated.
32 devices in a mesh: ctx: 8 (over z, x), dp: 4 (over y, core).
Axes of the slice: x: 2, y: 2, z: 4, core: 2. Of those that a mesh axis runs over, the one named last changes fastest.
Arguments:
- query: bfloat16 [4, 4096, 2048], P('dp', 'ctx'), may hold values from -0.75 to 0.75
- keys: bfloat16 [4, 4096, 2048], P('dp', 'ctx'), may hold values from -0.75 to 0.75
- values: bfloat16 [4, 4096, 2048], P('dp', 'ctx'), may hold values from -6 to 6
- upstream: bfloat16 [4, 4096, 2048], P('dp', 'ctx'), may hold values from -0.75 to 0.75
- out_weight: bfloat16 [2048, 2048], replicated, may hold values from -0.125 to 0.125
- log_decay: float32 [4, 4096, 16], P('dp', 'ctx'), may hold values from -0.9 to 0, as said below
- signs: int32 [4, 4096], P('dp', 'ctx'), may hold values 0 or 1
- magnitude: float32 [4, 4096], P('dp', 'ctx'), may hold values from 0.5 to 2
Outputs:
- grad_query: bfloat16 [4, 4096, 2048], P('dp', 'ctx')
- grad_keys: bfloat16 [4, 4096, 2048], P('dp', 'ctx')
- grad_values: bfloat16 [4, 4096, 2048], P('dp', 'ctx')
- grad_out_weight: float32 [2048, 2048], P(('ctx', 'dp'))
Inputs may be any that keep to these rules, and one draw needn't show every extreme that they name: `log_decay`: every entry is negative.
All inputs are finite; a program needn't handle non-finite values. No bound on the sum of `signs` on one device may be relied on, other than what follows from the above.
Results may differ from a plain program's by a relative error of at most 0.006.
Values sent between devices are 32-bit elements; how exact they have to be, the bound alone decides.
No kernel may reach another device: no remote copies, remote signals or barrier semaphores. Data moves between devices by JAX's collectives and lax.ppermute only.
A program may use at most 192 MiB of HBM per device.

v0:
```python
import jax
import jax.numpy as jnp
from jax import lax
from jax.sharding import PartitionSpec as P

LOCAL_HEADS = 16
HD = 128
BLOCK = 512


def carried_in(value, axis, join, neutral, backward):
    count, mine = (lax.axis_size(axis), lax.axis_index(axis))
    pieces = jax.tree.map(lambda part: lax.all_gather(part, axis), value)
    if backward:
        pieces = jax.tree.map(lambda part: part[::-1], pieces)
        mine = count - 1 - mine
    subtotal = jax.tree.map(
        lambda part, zero: jnp.full_like(part, 0) + jnp.asarray(zero, part.dtype), value, neutral
    )

    def turn(position, subtotal):
        longer = join(subtotal, jax.tree.map(lambda part: part[position], pieces))
        return jax.tree.map(lambda new, old: jnp.where(position < mine, new, old), longer, subtotal)

    return lax.fori_loop(0, count - 1, turn, subtotal)


def block_terms(query_block, key_block, value_block, dout_block, decay_block, scale, lower_mask):
    cumulate = jnp.cumsum(decay_block, axis=0)
    spread = cumulate.T[:, :, None] - cumulate.T[:, None, :]
    weight = jnp.where(lower_mask, jnp.exp(jnp.where(lower_mask, spread, 0.0)), 0.0)
    scores = jnp.einsum("thd,shd->hts", query_block, key_block, preferred_element_type=jnp.float32)
    dscores = jnp.einsum(
        "thd,shd->hts", dout_block, value_block, preferred_element_type=jnp.float32
    )
    probs = (scale * scores * weight).astype(jnp.bfloat16)
    dprobs = (scale * dscores * weight).astype(jnp.bfloat16)
    attend = jnp.einsum("hts,shd->thd", probs, value_block, preferred_element_type=jnp.float32)
    grad_q = jnp.einsum("hts,shd->thd", dprobs, key_block, preferred_element_type=jnp.float32)
    grad_k = jnp.einsum("hts,thd->shd", dprobs, query_block, preferred_element_type=jnp.float32)
    grad_v = jnp.einsum("hts,thd->shd", probs, dout_block, preferred_element_type=jnp.float32)
    growth = jnp.exp(cumulate)[:, :, None]
    remain = jnp.exp(cumulate[-1][None, :] - cumulate)[:, :, None]
    state_own = jnp.einsum(
        "shd,she->hde",
        key_block.astype(jnp.float32) * remain,
        value_block.astype(jnp.float32),
        precision=lax.Precision.HIGHEST,
    )
    back_own = jnp.einsum(
        "thd,the->hde",
        query_block.astype(jnp.float32) * growth,
        dout_block.astype(jnp.float32),
        precision=lax.Precision.HIGHEST,
    )
    return (attend, grad_q, grad_k, grad_v, state_own, back_own, cumulate[-1])


def local_terms(query_heads, key_heads, value_heads, dout_heads, decay_log, scale):
    lower_mask = (jnp.arange(BLOCK)[:, None] >= jnp.arange(BLOCK)[None, :])[None]
    attend, grad_q, grad_k, grad_v, state_end, back_end, last_total = block_terms(
        query_heads, key_heads, value_heads, dout_heads, decay_log, scale, lower_mask
    )
    return (attend, grad_q, grad_k, grad_v, state_end, back_end)


def chain_join(earlier, later):
    return (earlier[0] + later[0], jnp.exp(later[0])[:, None, None] * earlier[1] + later[1])


def on_device(query, keys, values, upstream, out_weight, log_decay, signs, magnitude):
    tokens = query.shape[1]
    width = query.shape[2]
    scale = HD ** (-0.5)
    advantage = (2 * signs[0] - 1).astype(jnp.float32) * magnitude[0]
    weighted = (advantage[:, None] * upstream[0].astype(jnp.float32)).astype(jnp.bfloat16)
    dout = lax.dot_general(
        weighted, out_weight, (((1,), (1,)), ((), ())), preferred_element_type=jnp.float32
    ).astype(jnp.bfloat16)

    def to_heads(array):
        return array.reshape(tokens, LOCAL_HEADS, HD)

    decay_here = log_decay[0]
    query_heads = to_heads(query[0])
    key_heads = to_heads(keys[0])
    value_heads = to_heads(values[0])
    dout_heads = to_heads(dout)
    attend, grad_q, grad_k, grad_v, state_end, back_end = local_terms(
        query_heads, key_heads, value_heads, dout_heads, decay_here, scale
    )
    running = jnp.cumsum(decay_here, axis=0)
    total = running[-1]
    identity = (jnp.zeros_like(total), jnp.zeros_like(state_end))
    state_in = carried_in((total, state_end), "ctx", chain_join, identity, False)[1]
    back_in = carried_in((total, back_end), "ctx", chain_join, identity, True)[1]
    query_f32 = query_heads.astype(jnp.float32)
    key_f32 = key_heads.astype(jnp.float32)
    value_f32 = value_heads.astype(jnp.float32)
    dout_f32 = dout_heads.astype(jnp.float32)
    growth = jnp.exp(running)[:, :, None]
    remain = jnp.exp(total[None, :] - running)[:, :, None]
    attend = attend + scale * growth * jnp.einsum(
        "thd,hde->the", query_f32, state_in, precision=lax.Precision.HIGHEST
    )
    grad_q = grad_q + scale * growth * jnp.einsum(
        "hde,the->thd", state_in, dout_f32, precision=lax.Precision.HIGHEST
    )
    grad_k = grad_k + scale * remain * jnp.einsum(
        "hde,she->shd", back_in, value_f32, precision=lax.Precision.HIGHEST
    )
    grad_v = grad_v + scale * remain * jnp.einsum(
        "hde,shd->she", back_in, key_f32, precision=lax.Precision.HIGHEST
    )
    attn = attend.reshape(tokens, width).astype(jnp.bfloat16)
    grad_weight = lax.psum_scatter(
        lax.dot_general(
            attn, weighted, (((0,), (0,)), ((), ())), preferred_element_type=jnp.float32
        ),
        ("ctx", "dp"),
        scatter_dimension=0,
        tiled=True,
    )
    shape_out = (1, tokens, width)
    return (
        grad_q.reshape(shape_out).astype(jnp.bfloat16),
        grad_k.reshape(shape_out).astype(jnp.bfloat16),
        grad_v.reshape(shape_out).astype(jnp.bfloat16),
        grad_weight,
    )


def solution(mesh):
    in_specs = (
        P("dp", "ctx", None),
        P("dp", "ctx", None),
        P("dp", "ctx", None),
        P("dp", "ctx", None),
        P(),
        P("dp", "ctx", None),
        P("dp", "ctx"),
        P("dp", "ctx"),
    )
    out_specs = (
        P("dp", "ctx", None),
        P("dp", "ctx", None),
        P("dp", "ctx", None),
        P(("ctx", "dp"), None),
    )
    return jax.shard_map(
        on_device, mesh=mesh, in_specs=in_specs, out_specs=out_specs, check_vma=False
    )
```

profile of v0, /device:TPU:11, one launch (start us, length us, event | category | flops | bytes accessed | tf_op | source)
XLA Modules:
  0.0 465.4 jit_solution(8758672777072301636)
XLA Ops:
  7.2 0.7 copy-done
  7.9 1.1 reduce-window.6
  9.1 0.2 slice_reduce_fusion
  9.3 0.2 slice_reduce_fusion.1
  9.5 0.1 broadcast_multiply_fusion
  9.6 2.9 copy.113
  12.5 4.6 copy.112
  17.1 4.9 %fusion.16 = f32[16,128,128]{2,1,0:T(8,128)} fusion(bf16[512,16,128]{0,2,1:T(8,128)(2,1)} %bitcast.141, bf16[512,16,128]{0,2,1:T(8,128)(2,1)S(1)} %bitcast.137, f32[512,16]{0,1:T(8,128)S(1)} %get-tuple-element.267), kind=kOutput, calls=%fused_computation.29 | convolution fusion | flops 1612709888 | bytes 5275648 | tf_op jit(solution)/shard_map/shd,she->hde/dot_general | solution.py:44
  22.1 9.9 %convolution_convert_fusion = bf16[512,2048]{1,0:T(8,128)(2,1)} fusion(bf16[2048,2048]{1,0:T(8,128)(2,1)} %param.16, bf16[1,512,2048]{2,1,0:T(8,128)(2,1)} %param.15, f32[512]{0:T(512)S(1)} %bitcast.153), kind=kOutput, calls=%fused_computation.32 | convolution fusion | flops 4299161600 | bytes 12584960 | tf_op jit(solution)/shard_map/dot_general | solution.py:77
  32.0 3.1 copy.111
  35.1 4.6 copy.114
  39.7 4.8 %fusion.13 = f32[16,128,128]{2,1,0:T(8,128)} fusion(bf16[512,16,128]{0,2,1:T(8,128)(2,1)S(1)} %bitcast.129, bf16[512,16,128]{0,2,1:T(8,128)(2,1)} %bitcast.133, f32[512,16]{0,1:T(8,128)S(1)} %get-tuple-element.268), kind=kOutput, calls=%fused_computation.26 | convolution fusion | flops 1612709888 | bytes 5275648 | tf_op jit(solution)/shard_map/thd,the->hde/dot_general | solution.py:50
  44.5 11.9 %all-gather.2 = f32[8,1,16]{2,1,0:T(1,128)S(1)} all-gather(f32[1,1,16]{2,1,0:T(1,128)S(1)} %bitcast.152), channel_id=1, replica_groups=mesh['ctx'=8,'dp'=4] {'ctx'}, dimensions={0}, use_global_device_ids=true | all-gather | bytes 576 | tf_op jit(solution)/shard_map/all_gather | solution.py:13
  56.5 8.0 %multiply_convert_fusion = bf16[16,512,512]{2,1,0:T(8,128)(2,1)S(1)} fusion(bf16[512,16,128]{0,2,1:T(8,128)(2,1)} %bitcast.134, bf16[512,16,128]{0,2,1:T(8,128)(2,1)} %bitcast.138, f32[16,512]{1,0:T(8,128)S(1)} %get-tuple-element.271, pred[512,512]{1,0:T(8,128)(4,1)S(1)} %iota_compare_fusion), kind=kOutput, calls=%fused_computation.6 | convolution fusion | flops 1098907648 | bytes 12877824 | tf_op jit(solution)/shard_map/thd,shd->hts/dot_general | solution.py:32
  64.6 3.2 copy-done.2
  67.8 4.8 %fusion.30 = f32[16,512,128]{1,2,0:T(8,128)} fusion(bf16[16,512,512]{2,1,0:T(8,128)(2,1)S(1)} %multiply_convert_fusion, bf16[512,16,128]{0,2,1:T(8,128)(2,1)S(1)} %bitcast.143), kind=kOutput, calls=%fused_computation.53 | convolution fusion | flops 1073741824 | bytes 14680064 | tf_op jit(solution)/shard_map/hts,shd->thd/dot_general | solution.py:38
  72.6 72.6 %all-gather.6.cloned.1.call-done = f32[128,128,128]{2,1,0:T(8,128)} async-done(((f32[16,128,128]{2,1,0:T(8,128)}), f32[128,128,128]{2,1,0:T(8,128)}) %all-gather.6.cloned.1.call-update) | async-done | bytes 8388624 | tf_op jit(solution)/shard_map/all_gather | solution.py:13
  145.2 10.6 %while.28 = (s32[]{:T(128)}, f32[16,128,128]{2,1,0:T(8,128)S(1)}, s32[]{:T(128)}, f32[8,16]{1,0:T(8,128)S(1)}, f32[8,16,128,128]{3,2,1,0:T(8,128)}, /*index=5*/s32[]{:T(128)}, s32[]{:T(128)}) while((s32[]{:T(128)}, f32[16,128,128]{2,1,0:T(8,128)S(1)}, s32[]{:T(128)}, f32[8,16]{1,0:T(8,128)S(1)}, f32[8,16,128,128]{3,2,1,0:T(8,128)}, ...), condition=%wide.region_3.4_spmd.clone, body=%wide.region_2.3_spmd.clone.sunk | while | flops 1048580 | bytes 3146033 | solution.py:25
  145.2 1.6 fusion.59
  146.9 1.5 fusion.59
  148.4 1.5 fusion.59
  149.9 1.5 fusion.59
  151.4 1.5 fusion.59
  152.9 1.5 fusion.59
  154.4 1.5 fusion.59
  155.9 4.9 %fusion.6 = bf16[512,16,128]{0,2,1:T(8,128)(2,1)S(1)} fusion(f32[16,512,128]{1,2,0:T(8,128)} %fusion.30, f32[16,128,128]{2,1,0:T(8,128)S(1)} %get-tuple-element.192, bf16[512,16,128]{0,2,1:T(8,128)(2,1)S(1)} %bitcast.135, f32[512,16]{0,1:T(8,128)S(1)} %get-tuple-element.269), kind=kOutput, calls=%fused_computation.16 | convolution fusion | flops 1613758464 | bytes 9469952 | tf_op jit(solution)/shard_map/thd,hde->the/dot_general | solution.py:103
  160.8 8.3 %fusion.20 = f32[2048,2048]{1,0:T(8,128)} fusion(bf16[512,2048]{0,1:T(8,128)(2,1)S(1)} %bitcast.150, bf16[1,512,2048]{2,1,0:T(8,128)(2,1)S(1)} %copy-done.13, f32[512]{0:T(512)S(1)} %bitcast.154), kind=kOutput, calls=%fused_computation.34 | convolution fusion | flops 4298113024 | bytes 20973568 | tf_op jit(solution)/shard_map/dot_general | solution.py:117
  169.2 7.6 %fusion.29 = f32[16,128,512]{2,1,0:T(8,128)} fusion(bf16[512,16,128]{0,2,1:T(8,128)(2,1)} %bitcast.130, bf16[16,512,512]{2,1,0:T(8,128)(2,1)} %copy-done.2), kind=kOutput, calls=%fused_computation.52 | convolution fusion | flops 1073741824 | bytes 14680064 | tf_op jit(solution)/shard_map/hts,thd->shd/dot_general | solution.py:41
  176.7 6.5 %multiply_convert_fusion.1 = bf16[16,512,512]{2,1,0:T(8,128)(2,1)S(1)} fusion(bf16[512,16,128]{0,2,1:T(8,128)(2,1)S(1)} %bitcast.132, bf16[512,16,128]{0,2,1:T(8,128)(2,1)S(1)} %bitcast.144, f32[16,512]{1,0:T(8,128)S(1)} %get-tuple-element.271, pred[512,512]{1,0:T(8,128)(4,1)S(1)} %iota_compare_fusion), kind=kOutput, calls=%fused_computation.7 | convolution fusion | flops 1098907648 | bytes 12877824 | tf_op jit(solution)/shard_map/thd,shd->hts/dot_general | solution.py:33
  183.3 3.2 fusion.31
  186.5 4.8 %fusion.28 = f32[16,512,128]{1,2,0:T(8,128)} fusion(bf16[16,512,512]{2,1,0:T(8,128)(2,1)S(1)} %multiply_convert_fusion.1, bf16[512,16,128]{0,2,1:T(8,128)(2,1)S(1)} %bitcast.140), kind=kOutput, calls=%fused_computation.51 | convolution fusion | flops 1073741824 | bytes 14680064 | tf_op jit(solution)/shard_map/hts,shd->thd/dot_general | solution.py:39
  191.2 79.2 %all-gather.8.cloned.1.call-done = f32[128,128,128]{2,1,0:T(8,128)} async-done(((f32[16,128,128]{2,1,0:T(8,128)}), f32[128,128,128]{2,1,0:T(8,128)}) %all-gather.8.cloned.1.call-update) | async-done | bytes 8388624 | tf_op jit(solution)/shard_map/all_gather | solution.py:13
  270.5 7.7 %rev.7 = f32[8,16,128,128]{3,2,1,0:T(8,128)} reverse(f32[8,16,128,128]{3,2,1,0:T(8,128)} %bitcast.145), dimensions={0} | reverse | bytes 16777216 | tf_op jit(solution)/shard_map/rev | solution.py:15
  278.2 10.5 %while.29 = (s32[]{:T(128)}, f32[16,128,128]{2,1,0:T(8,128)S(1)}, s32[]{:T(128)}, f32[8,16]{1,0:T(8,128)S(1)}, f32[8,16,128,128]{3,2,1,0:T(8,128)}, /*index=5*/s32[]{:T(128)}, s32[]{:T(128)}) while((s32[]{:T(128)}, f32[16,128,128]{2,1,0:T(8,128)S(1)}, s32[]{:T(128)}, f32[8,16]{1,0:T(8,128)S(1)}, f32[8,16,128,128]{3,2,1,0:T(8,128)}, ...), condition=%wide.region_5.6_spmd.clone, body=%wide.region_4.5_spmd.clone.sunk | while | flops 1048580 | bytes 3146033 | solution.py:25
  278.2 1.5 fusion.60
  279.7 1.5 fusion.60
  281.2 1.5 fusion.60
  282.7 1.5 fusion.60
  284.2 1.5 fusion.60
  285.7 1.5 fusion.60
  287.2 1.5 fusion.60
  288.7 6.2 %fusion.10 = bf16[512,16,128]{0,2,1:T(8,128)(2,1)} fusion(f32[16,512,128]{1,2,0:T(8,128)} %fusion.31, f32[16,128,128]{2,1,0:T(8,128)S(1)} %get-tuple-element.193, bf16[512,16,128]{0,2,1:T(8,128)(2,1)} %bitcast.142, f32[512,16]{0,1:T(8,128)S(1)} %get-tuple-element.266), kind=kOutput, calls=%fused_computation.22 | convolution fusion | flops 1613758464 | bytes 9469952 | tf_op jit(solution)/shard_map/hde,she->shd/dot_general | solution.py:109
  294.9 3.9 copy.107
  298.8 6.2 %fusion.12 = bf16[512,16,128]{0,2,1:T(8,128)(2,1)} fusion(f32[16,512,128]{1,2,0:T(8,128)} %fusion.28, bf16[512,16,128]{0,2,1:T(8,128)(2,1)} %bitcast.131, f32[16,128,128]{2,1,0:T(8,128)S(1)} %get-tuple-element.192, f32[512,16]{0,1:T(8,128)S(1)} %get-tuple-element.269), kind=kOutput, calls=%fused_computation.25 | convolution fusion | flops 1613758464 | bytes 9469952 | tf_op jit(solution)/shard_map/hde,the->thd/dot_general | solution.py:106
  305.0 3.9 copy.106
  309.0 6.2 %fusion.8 = bf16[512,16,128]{0,2,1:T(8,128)(2,1)} fusion(f32[16,128,512]{2,1,0:T(8,128)} %fusion.29, f32[16,128,128]{2,1,0:T(8,128)S(1)} %get-tuple-element.193, bf16[512,16,128]{0,2,1:T(8,128)(2,1)} %bitcast.139, f32[512,16]{0,1:T(8,128)S(1)} %get-tuple-element.266), kind=kOutput, calls=%fused_computation.19 | convolution fusion | flops 1613758464 | bytes 9469952 | tf_op jit(solution)/shard_map/hde,shd->she/dot_general | solution.py:112
  315.2 3.9 copy.108
  319.1 139.8 %reduce-scatter.2.cloned.1.call-done = f32[64,2048]{1,0:T(8,128)} async-done(((f32[2048,2048]{1,0:T(8,128)}), f32[64,2048]{1,0:T(8,128)}) %reduce-scatter.2.cloned.1.call-update) | async-done | bytes 524304 | tf_op jit(solution)/shard_map/reduce_scatter | solution.py:116
  (55 shorter events, 0.6 us)
Async XLA Ops:
  7.2 0.8 copy-start
  7.2 138.0 %all-gather.6.cloned.1.call-start = ((), (), s32[]{:S(2)}) async-start(), calls=%async_computation.2 | async-start | bytes 9437184 | tf_op jit(solution)/shard_map/all_gather | solution.py:13
  12.5 9.5 %copy-start.7 = (bf16[1,512,2048]{1,2,0:T(8,128)(2,1)}, bf16[1,512,2048]{1,2,0:T(8,128)(2,1)S(1)}, u32[]{:S(2)}) copy-start(bf16[1,512,2048]{1,2,0:T(8,128)(2,1)S(1)} %copy.113) | copy-start | bytes 6291460
  17.1 5.0 %copy-start.11 = (f32[1,512]{1,0:T(1,128)S(1)}, f32[1,512]{1,0:T(1,128)}, u32[]{:S(2)}) copy-start(f32[1,512]{1,0:T(1,128)} %param.19) | copy-start | bytes 6148
  17.1 5.0 %copy-start.12 = (s32[1,512]{1,0:T(1,128)S(1)}, s32[1,512]{1,0:T(1,128)}, u32[]{:S(2)}) copy-start(s32[1,512]{1,0:T(1,128)} %param.18) | copy-start | bytes 6148
  22.0 248.4 %all-gather.8.cloned.1.call-start = ((), (), s32[]{:S(2)}) async-start(), calls=%async_computation.3 | async-start | bytes 9437184 | tf_op jit(solution)/shard_map/all_gather | solution.py:13
  35.1 9.4 %copy-start.3 = (bf16[512,2048]{0,1:T(8,128)(2,1)}, bf16[512,2048]{0,1:T(8,128)(2,1)S(1)}, u32[]{:S(2)}) copy-start(bf16[512,2048]{0,1:T(8,128)(2,1)S(1)} %copy.111) | copy-start | bytes 6291460
  44.5 414.4 %reduce-scatter.2.cloned.1.call-start = ((), (), s32[]{:S(2)}) async-start(), calls=%async_computation.1 | async-start | bytes 17301504 | tf_op jit(solution)/shard_map/reduce_scatter | solution.py:116
  56.5 11.3 %copy-start.9 = (bf16[1,512,2048]{1,2,0:T(8,128)(2,1)S(1)}, bf16[1,512,2048]{1,2,0:T(8,128)(2,1)}, u32[]{:S(2)}) copy-start(bf16[1,512,2048]{1,2,0:T(8,128)(2,1)} %copy.112) | copy-start | bytes 6291460
  64.6 3.2 copy-start.2
  145.2 10.7 %copy-start.5 = (bf16[1,512,2048]{1,2,0:T(8,128)(2,1)S(1)}, bf16[1,512,2048]{1,2,0:T(8,128)(2,1)}, u32[]{:S(2)}) copy-start(bf16[1,512,2048]{1,2,0:T(8,128)(2,1)} %copy.114) | copy-start | bytes 6291460
  155.9 4.9 %copy-start.13 = (bf16[1,512,2048]{2,1,0:T(8,128)(2,1)S(1)}, bf16[1,512,2048]{2,1,0:T(8,128)(2,1)}, u32[]{:S(2)}) copy-start(bf16[1,512,2048]{2,1,0:T(8,128)(2,1)} %param.15) | copy-start | bytes 6291460
  169.1 7.6 %copy-start.4 = (bf16[512,2048]{0,1:T(8,128)(2,1)S(1)}, bf16[512,2048]{0,1:T(8,128)(2,1)}, u32[]{:S(2)}) copy-start(bf16[512,2048]{0,1:T(8,128)(2,1)} %copy-done.3) | copy-start | bytes 6291460
  169.2 7.6 %copy-start.10 = (bf16[1,512,2048]{1,2,0:T(8,128)(2,1)S(1)}, bf16[1,512,2048]{1,2,0:T(8,128)(2,1)}, u32[]{:S(2)}) copy-start(bf16[1,512,2048]{1,2,0:T(8,128)(2,1)} %copy.112) | copy-start | bytes 6291460
  176.7 6.5 %copy-start.6 = (bf16[1,512,2048]{1,2,0:T(8,128)(2,1)S(1)}, bf16[1,512,2048]{1,2,0:T(8,128)(2,1)}, u32[]{:S(2)}) copy-start(bf16[1,512,2048]{1,2,0:T(8,128)(2,1)} %copy.114) | copy-start | bytes 6291460
  183.2 3.2 copy-start.8
  309.0 149.9 %copy-start.1 = (f32[1,512,16]{1,2,0:T(8,128)S(1)}, f32[1,512,16]{1,2,0:T(8,128)}, u32[]{:S(2)}) copy-start(f32[1,512,16]{1,2,0:T(8,128)} %param.17) | copy-start | bytes 98308
Sparse Core Ops, SparseCore 0:
  22.2 122.9 all-gather.5
  147.3 123.1 all-gather.7
  273.3 185.4 reduce-scatter.1
where the time goes:
time: 468 us; the launch traced here: 465 us
  waiting for transfers between devices  292 us (62%)
  matrix products  86.2 us (18%)
  local copies, waits for them, and re-layouts  39.1 us (8%)
  other arithmetic  22.1 us (5%)
  between operations  14 us (3%)
  blocking collectives  11.9 us (3%)
    all_gather x2, waiting for transfers between devices, carried_in(): pieces = jax.tree.map(lambda part: lax.all_gather(part, axis), value)  152 us
    reduce_scatter x1, waiting for transfers between devices, on_device(): lax.psum_scatter(lax.dot_general(attn, weighted, (((0,), (0,)), ((), ()))...  140 us
    select_n x14, other arithmetic, turn(): jnp.where(position < mine, new, old)  20.6 us
    unnamed x31, local copies, waits for them, and re-layouts  15.8 us
    another operation x3, local copies, waits for them, and re-layouts, to_heads(): return array.reshape(tokens, LOCAL_HEADS, HD)  12 us
    all_gather x1, blocking collectives, carried_in(): pieces = jax.tree.map(lambda part: lax.all_gather(part, axis), value)  11.9 us
    dot_general x1, matrix products, on_device(): lax.dot_general(weighted, out_weight, (((1,), (1,)), ((), ())), preferred...  9.89 us
  transfers between devices with their start and end apart: 3, of which 3 were waited for; matrix products, arithmetic and copies ran while one was open for 28% of the time, Pallas kernels for 0%

commit v1 on v0

--- a/solution.py
+++ b/solution.py
@@ -8,21 +8,22 @@
 BLOCK = 512
 
 
-def carried_in(value, axis, join, neutral, backward):
-    count, mine = (lax.axis_size(axis), lax.axis_index(axis))
-    pieces = jax.tree.map(lambda part: lax.all_gather(part, axis), value)
-    if backward:
-        pieces = jax.tree.map(lambda part: part[::-1], pieces)
-        mine = count - 1 - mine
-    subtotal = jax.tree.map(
-        lambda part, zero: jnp.full_like(part, 0) + jnp.asarray(zero, part.dtype), value, neutral
-    )
-
-    def turn(position, subtotal):
-        longer = join(subtotal, jax.tree.map(lambda part: part[position], pieces))
-        return jax.tree.map(lambda new, old: jnp.where(position < mine, new, old), longer, subtotal)
-
-    return lax.fori_loop(0, count - 1, turn, subtotal)
+def carried_in(value, axis, join, backward):
+    count = lax.axis_size(axis)
+    step = -1 if backward else 1
+    partial = value
+    gathered = None
+    distance = 1
+    while distance < count:
+        pairs = [(i, i + step * distance) for i in range(count) if 0 <= i + step * distance < count]
+        arrived = jax.tree.map(lambda part: lax.ppermute(part, axis, pairs), partial)
+        gathered = arrived if gathered is None else join(arrived, gathered)
+        if distance * 2 < count:
+            partial = join(arrived, partial)
+        distance *= 2
+    if gathered is None:
+        gathered = jax.tree.map(jnp.zeros_like, value)
+    return gathered
 
 
 def block_terms(query_block, key_block, value_block, dout_block, decay_block, scale, lower_mask):
@@ -91,9 +92,8 @@
     )
     running = jnp.cumsum(decay_here, axis=0)
     total = running[-1]
-    identity = (jnp.zeros_like(total), jnp.zeros_like(state_end))
-    state_in = carried_in((total, state_end), "ctx", chain_join, identity, False)[1]
-    back_in = carried_in((total, back_end), "ctx", chain_join, identity, True)[1]
+    state_in = carried_in((total, state_end), "ctx", chain_join, False)[1]
+    back_in = carried_in((total, back_end), "ctx", chain_join, True)[1]
     query_f32 = query_heads.astype(jnp.float32)
     key_f32 = key_heads.astype(jnp.float32)
     value_f32 = value_heads.astype(jnp.float32)

time: 468 us -> 391 us (0.84)
  waiting for transfers between devices: 292 us -> 232 us
  starting transfers between devices: 0.12 us -> 27 us
  blocking collectives: 11.9 us -> 0 us
  matrix products: 86.2 us -> 74.6 us
  local copies, waits for them, and re-layouts: 39.1 us -> 28 us
  other arithmetic: 22.1 us -> 13.3 us
    all_gather x2 -> x0, waiting for transfers between devices: 152 us -> none  [carried_in(): pieces = jax.tree.map(lambda part: lax.all_gather(part, axis), value)]
    ppermute x0 -> x10, waiting for transfers between devices: none -> 91.3 us  [carried_in(): lax.ppermute(part, axis, pairs)]
    ppermute x0 -> x10, starting transfers between devices: none -> 27 us  [carried_in(): lax.ppermute(part, axis, pairs)]
    select_n x14 -> x0, other arithmetic: 20.6 us -> none  [turn(): jnp.where(position < mine, new, old)]
    all_gather x1 -> x0, blocking collectives: 11.9 us -> none  [carried_in(): pieces = jax.tree.map(lambda part: lax.all_gather(part, axis), value)]
    add x0 -> x5, other arithmetic: none -> 11.8 us  [chain_join(): jnp.exp(later[0])[:, None, None] * earlier[1] + later[1]]
    rev x2 -> x0, local copies, waits for them, and re-layouts: 7.72 us -> none  [carried_in(): pieces = jax.tree.map(lambda part: part[::-1], pieces)]
    unnamed x31 -> x51, local copies, waits for them, and re-layouts: 15.8 us -> 14.1 us
  transfers between devices with their start and end apart: 3 -> 11, of which waited for: 3 -> 6; matrix products, arithmetic and copies ran while one was open for 28% -> 21% of each run, Pallas kernels for 0% -> 0%
where the time goes in v1:
time: 391 us; the launch traced here: 390 us
  waiting for transfers between devices  232 us (59%)
  matrix products  74.6 us (19%)
  local copies, waits for them, and re-layouts  28 us (7%)
  starting transfers between devices  27 us (7%)
  between operations  14.5 us (4%)
  other arithmetic  13.3 us (3%)
    reduce_scatter x1, waiting for transfers between devices, on_device(): lax.psum_scatter(lax.dot_general(attn, weighted, (((0,), (0,)), ((), ()))...  141 us
    ppermute x10, waiting for transfers between devices, carried_in(): lax.ppermute(part, axis, pairs)  91.3 us
    ppermute x10, starting transfers between devices, carried_in(): lax.ppermute(part, axis, pairs)  27 us
    unnamed x51, local copies, waits for them, and re-layouts  14.1 us
    add x5, other arithmetic, chain_join(): jnp.exp(later[0])[:, None, None] * earlier[1] + later[1]  11.8 us
    another operation x3, local copies, waits for them, and re-layouts, to_heads(): return array.reshape(tokens, LOCAL_HEADS, HD)  10.7 us
    dot_general x1, matrix products, on_device(): lax.dot_general(weighted, out_weight, (((1,), (1,)), ((), ())), preferred...  9.19 us
    dot_general x1, matrix products, block_terms(): jnp.einsum('hts,shd->thd', dprobs, key_block, preferred_element_type=jnp....  8.27 us
  transfers between devices with their start and end apart: 11, of which 6 were waited for; matrix products, arithmetic and copies ran while one was open for 21% of the time, Pallas kernels for 0%

profile of v1, /device:TPU:11, one launch (start us, length us, event | category | flops | bytes accessed | tf_op | source)
XLA Modules:
  0.0 389.8 jit_solution(14930713944578124259)
XLA Ops:
  7.2 2.9 copy.89
  10.1 1.2 reduce-window.6
  11.3 0.2 slice_reduce_fusion
  11.6 3.9 %copy.90 = bf16[1,512,2048]{1,2,0:T(8,128)(2,1)} copy(bf16[1,512,2048]{2,1,0:T(8,128)(2,1)} %param.9) | data formatting | bytes 4194304 | tf_op jit(solution)/shard_map/reshape;squeeze | solution.py:83
  15.5 0.2 slice_reduce_fusion.1
  15.7 0.1 broadcast_multiply_fusion
  15.8 4.9 %fusion.14 = f32[16,128,128]{2,1,0:T(8,128)} fusion(bf16[512,16,128]{0,2,1:T(8,128)(2,1)S(1)} %bitcast.115, bf16[512,16,128]{0,2,1:T(8,128)(2,1)} %bitcast.119, f32[512,16]{0,1:T(8,128)S(1)} %get-tuple-element.17), kind=kOutput, calls=%fused_computation.23 | convolution fusion | flops 1612709888 | bytes 5275648 | tf_op jit(solution)/shard_map/shd,she->hde/dot_general | solution.py:45
  20.7 3.2 collective-permute-start.2
  23.9 9.2 %convolution_convert_fusion = bf16[512,2048]{1,0:T(8,128)(2,1)} fusion(bf16[2048,2048]{1,0:T(8,128)(2,1)} %param.12, bf16[1,512,2048]{2,1,0:T(8,128)(2,1)S(1)} %copy-done.20, f32[512]{0:T(512)S(1)} %bitcast.127), kind=kOutput, calls=%fused_computation.26 | convolution fusion | flops 4299161600 | bytes 12584960 | tf_op jit(solution)/shard_map/dot_general | solution.py:78
  33.1 2.9 copy.88
  36.0 3.9 %copy.91 = bf16[1,512,2048]{1,2,0:T(8,128)(2,1)} copy(bf16[1,512,2048]{2,1,0:T(8,128)(2,1)} %param.8) | data formatting | bytes 4194304 | tf_op jit(solution)/shard_map/reshape;squeeze | solution.py:83
  39.9 3.8 fusion.11
  43.7 2.1 collective-permute-start.7
  45.8 3.1 collective-permute-start.5
  48.9 3.1 collective-permute-start
  52.0 18.2 %collective-permute-done.5 = f32[16]{0:T(128)S(1)} collective-permute-done((f32[16]{0:T(128)S(1)}, f32[16]{0:T(128)S(1)}, u32[]{:S(2)}, u32[]{:S(2)}) %collective-permute-start.5) | collective-permute-done | bytes 96 | tf_op jit(solution)/shard_map/ppermute | solution.py:19
  70.3 3.4 multiply_add_fusion.1
  73.7 3.2 collective-permute-start.3
  76.9 0.1 iota_compare_fusion
  77.0 21.3 %collective-permute-done.3 = f32[16,128,128]{2,1,0:T(8,128)S(1)} collective-permute-done((f32[16,128,128]{2,1,0:T(8,128)S(1)}, f32[16,128,128]{2,1,0:T(8,128)S(1)}, u32[]{:S(2)}, u32[]{:S(2)}) %collective-permute-start.3) | collective-permute-done | bytes 1048608 | tf_op jit(solution)/shard_map/ppermute | solution.py:19
  98.2 1.4 multiply_add_fusion.2
  99.7 4.2 %collective-permute-start.4 = (f32[16,128,128]{2,1,0:T(8,128)}, f32[16,128,128]{2,1,0:T(8,128)}, u32[]{:S(2)}, u32[]{:S(2)}) collective-permute-start(f32[16,128,128]{2,1,0:T(8,128)} %multiply_add_fusion.2), channel_id=1, source_target_pairs={{0,16},{4,20},{8,24},{12,28},{1,17},{5,21},{9,25},{13,29},{2,18},{... | collective-permute-start | bytes 3145736 | tf_op jit(solution)/shard_map/ppermute | solution.py:19
  103.9 6.3 %multiply_convert_fusion = bf16[16,512,512]{2,1,0:T(8,128)(2,1)S(1)} fusion(bf16[512,16,128]{0,2,1:T(8,128)(2,1)S(1)} %bitcast.112, bf16[512,16,128]{0,2,1:T(8,128)(2,1)S(1)} %bitcast.120, f32[16,512]{1,0:T(8,128)S(1)} %get-tuple-element.25, pred[512,512]{1,0:T(8,128)(4,1)S(1)} %iota_compare_fusion), kind=kOutput, calls=%fused_computation | convolution fusion | flops 1098907648 | bytes 12877824 | tf_op jit(solution)/shard_map/thd,shd->hts/dot_general | solution.py:33
  110.2 2.1 collective-permute-start.1
  112.3 4.8 %fusion.30 = f32[16,512,128]{1,2,0:T(8,128)} fusion(bf16[16,512,512]{2,1,0:T(8,128)(2,1)S(1)} %multiply_convert_fusion, bf16[512,16,128]{0,2,1:T(8,128)(2,1)S(1)} %bitcast.117), kind=kOutput, calls=%fused_computation.57 | convolution fusion | flops 1073741824 | bytes 14680064 | tf_op jit(solution)/shard_map/hts,shd->thd/dot_general | solution.py:39
  117.1 30.5 %collective-permute-done.1 = f32[16]{0:T(128)S(1)} collective-permute-done((f32[16]{0:T(128)S(1)}, f32[16]{0:T(128)S(1)}, u32[]{:S(2)}, u32[]{:S(2)}) %collective-permute-start.1) | collective-permute-done | bytes 96 | tf_op jit(solution)/shard_map/ppermute | solution.py:19
  147.6 2.1 add_add_fusion.1
  149.8 2.3 fusion.4
  152.0 8.2 %fusion.18 = f32[2048,2048]{1,0:T(8,128)} fusion(bf16[512,2048]{0,1:T(8,128)(2,1)S(1)} %bitcast.126, bf16[1,512,2048]{2,1,0:T(8,128)(2,1)S(1)} %copy-done.21, f32[512]{0:T(512)S(1)} %bitcast.128), kind=kOutput, calls=%fused_computation.28 | convolution fusion | flops 4298113024 | bytes 20973568 | tf_op jit(solution)/shard_map/dot_general | solution.py:117
  160.3 7.9 %multiply_convert_fusion.1 = bf16[16,512,512]{2,1,0:T(8,128)(2,1)S(1)} fusion(bf16[512,16,128]{0,2,1:T(8,128)(2,1)S(1)} %bitcast.108, bf16[512,16,128]{0,2,1:T(8,128)(2,1)} %bitcast.116, f32[16,512]{1,0:T(8,128)S(1)} %get-tuple-element.25, pred[512,512]{1,0:T(8,128)(4,1)S(1)} %iota_compare_fusion), kind=kOutput, calls=%fused_computation.1 | convolution fusion | flops 1098907648 | bytes 12877824 | tf_op jit(solution)/shard_map/thd,shd->hts/dot_general | solution.py:34
  168.2 2.3 collective-permute-start.8
  170.5 1.9 copy-done.3
  172.5 3.4 fusion.31
  175.9 8.3 %fusion.28 = f32[16,512,128]{1,2,0:T(8,128)} fusion(bf16[16,512,512]{2,1,0:T(8,128)(2,1)} %copy-done.3, bf16[512,16,128]{0,2,1:T(8,128)(2,1)S(1)} %bitcast.121), kind=kOutput, calls=%fused_computation.55 | convolution fusion | flops 1073741824 | bytes 14680064 | tf_op jit(solution)/shard_map/hts,shd->thd/dot_general | solution.py:40
  184.1 1.9 collective-permute-start.6
  186.0 8.3 %collective-permute-done.8 = f32[16,128,128]{2,1,0:T(8,128)} collective-permute-done((f32[16,128,128]{2,1,0:T(8,128)}, f32[16,128,128]{2,1,0:T(8,128)}, u32[]{:S(2)}, u32[]{:S(2)}) %collective-permute-start.8) | collective-permute-done | bytes 1048608 | tf_op jit(solution)/shard_map/ppermute | solution.py:19
  194.3 2.7 multiply_add_fusion
  197.0 1.8 collective-permute-start.9
  198.8 3.2 fusion.29
  202.1 3.5 fusion.10
  205.6 4.1 %copy.83 = bf16[1,512,2048]{2,1,0:T(8,128)(2,1)} copy(bf16[1,512,2048]{1,2,0:T(8,128)(2,1)} %bitcast.123) | data formatting | bytes 4194304
  209.7 13.0 %collective-permute-done.9 = f32[16,128,128]{2,1,0:T(8,128)} collective-permute-done((f32[16,128,128]{2,1,0:T(8,128)}, f32[16,128,128]{2,1,0:T(8,128)}, u32[]{:S(2)}, u32[]{:S(2)}) %collective-permute-start.9) | collective-permute-done | bytes 1048608 | tf_op jit(solution)/shard_map/ppermute | solution.py:19
  222.7 2.2 add_add_fusion
  224.9 3.3 fusion.8
  228.2 4.1 %copy.84 = bf16[1,512,2048]{2,1,0:T(8,128)(2,1)} copy(bf16[1,512,2048]{1,2,0:T(8,128)(2,1)} %bitcast.125) | data formatting | bytes 4194304
  232.3 5.6 %fusion.6 = bf16[512,16,128]{0,2,1:T(8,128)(2,1)} fusion(f32[16,128,512]{2,1,0:T(8,128)} %fusion.29, f32[16,128,128]{2,1,0:T(8,128)S(1)} %add_add_fusion, bf16[512,16,128]{0,2,1:T(8,128)(2,1)S(1)} %bitcast.122, f32[512,16]{0,1:T(8,128)S(1)} %get-tuple-element.16), kind=kOutput, calls=%fused_computation.13 | convolution fusion | flops 1613758464 | bytes 9469952 | tf_op jit(solution)/shard_map/hde,shd->she/dot_general | solution.py:112
  237.9 3.9 %copy.85 = bf16[1,512,2048]{2,1,0:T(8,128)(2,1)} copy(bf16[1,512,2048]{1,2,0:T(8,128)(2,1)} %bitcast.124) | data formatting | bytes 4194304
  241.8 141.2 %reduce-scatter.2.cloned.1.call-done = f32[64,2048]{1,0:T(8,128)} async-done(((f32[2048,2048]{1,0:T(8,128)}), f32[64,2048]{1,0:T(8,128)}) %reduce-scatter.2.cloned.1.call-update) | async-done | bytes 524304 | tf_op jit(solution)/shard_map/reduce_scatter | solution.py:116
  (63 shorter events, 0.3 us)
Async XLA Ops:
  7.2 2.9 copy-start
  7.2 375.8 %reduce-scatter.2.cloned.1.call-start = ((), (), s32[]{:S(2)}) async-start(), calls=%async_computation.1 | async-start | bytes 17301504 | tf_op jit(solution)/shard_map/reduce_scatter | solution.py:116
  10.1 10.6 %copy-start.6 = (bf16[1,512,2048]{1,2,0:T(8,128)(2,1)}, bf16[1,512,2048]{1,2,0:T(8,128)(2,1)S(1)}, u32[]{:S(2)}) copy-start(bf16[1,512,2048]{1,2,0:T(8,128)(2,1)S(1)} %copy.89) | copy-start | bytes 6291460
  11.6 12.3 %copy-start.18 = (f32[1,512]{1,0:T(1,128)S(1)}, f32[1,512]{1,0:T(1,128)}, u32[]{:S(2)}) copy-start(f32[1,512]{1,0:T(1,128)} %param.15) | copy-start | bytes 6148
  11.6 12.3 %copy-start.19 = (s32[1,512]{1,0:T(1,128)S(1)}, s32[1,512]{1,0:T(1,128)}, u32[]{:S(2)}) copy-start(s32[1,512]{1,0:T(1,128)} %param.14) | copy-start | bytes 6148
  15.5 8.4 %copy-start.20 = (bf16[1,512,2048]{2,1,0:T(8,128)(2,1)S(1)}, bf16[1,512,2048]{2,1,0:T(8,128)(2,1)}, u32[]{:S(2)}) copy-start(bf16[1,512,2048]{2,1,0:T(8,128)(2,1)} %param.11) | copy-start | bytes 6291460
  20.7 49.5 %collective-permute-start.2 = (f32[16,128,128]{2,1,0:T(8,128)}, f32[16,128,128]{2,1,0:T(8,128)S(1)}, u32[]{:S(2)}, u32[]{:S(2)}) collective-permute-start(f32[16,128,128]{2,1,0:T(8,128)} %fusion.14), channel_id=1, source_target_pairs={{0,4},{4,8},{8,12},{12,16},{16,20},{20,24},{24,28},{1,5},{5,9},{9,... | collective-permute-start | bytes 3145736 | tf_op jit(solution)/shard_map/ppermute | solution.py:19
  43.7 26.5 %collective-permute-start.7 = (f32[16,128,128]{2,1,0:T(8,128)S(1)}, f32[16,128,128]{2,1,0:T(8,128)S(1)}, u32[]{:S(2)}, u32[]{:S(2)}) collective-permute-start(f32[16,128,128]{2,1,0:T(8,128)S(1)} %fusion.11), channel_id=1, source_target_pairs={{4,0},{8,4},{12,8},{16,12},{20,16},{24,20},{28,24},{5,1},{9,5},{13... | collective-permute-start | bytes 3145736 | tf_op jit(solution)/shard_map/ppermute | solution.py:19
  45.8 24.4 %collective-permute-start.5 = (f32[16]{0:T(128)S(1)}, f32[16]{0:T(128)S(1)}, u32[]{:S(2)}, u32[]{:S(2)}) collective-permute-start(f32[16]{0:T(128)S(1)} %slice_reduce_fusion.1), channel_id=1, source_target_pairs={{4,0},{8,4},{12,8},{16,12},{20,16},{24,20},{28,24},{5,1},{9,5},{13... | collective-permute-start | bytes 200 | tf_op jit(solution)/shard_map/ppermute | solution.py:19
  48.9 21.3 %collective-permute-start = (f32[16]{0:T(128)S(1)}, f32[16]{0:T(128)S(1)}, u32[]{:S(2)}, u32[]{:S(2)}) collective-permute-start(f32[16]{0:T(128)S(1)} %slice_reduce_fusion.1), channel_id=1, source_target_pairs={{0,4},{4,8},{8,12},{12,16},{16,20},{20,24},{24,28},{1,5},{5,9},{9,... | collective-permute-start | bytes 200 | tf_op jit(solution)/shard_map/ppermute | solution.py:19
  70.2 29.5 %copy-start.16 = (f32[16,128,128]{2,1,0:T(8,128)}, f32[16,128,128]{2,1,0:T(8,128)S(1)}, u32[]{:S(2)}) copy-start(f32[16,128,128]{2,1,0:T(8,128)S(1)} %collective-permute-done.2) | copy-start | bytes 3145732
  70.2 29.4 %copy-start.15 = (f32[16,128,128]{2,1,0:T(8,128)}, f32[16,128,128]{2,1,0:T(8,128)S(1)}, u32[]{:S(2)}) copy-start(f32[16,128,128]{2,1,0:T(8,128)S(1)} %collective-permute-done.7) | copy-start | bytes 3145732
  70.2 33.6 %copy-start.4 = (bf16[1,512,2048]{1,2,0:T(8,128)(2,1)S(1)}, bf16[1,512,2048]{1,2,0:T(8,128)(2,1)}, u32[]{:S(2)}) copy-start(bf16[1,512,2048]{1,2,0:T(8,128)(2,1)} %copy.91) | copy-start | bytes 6291460
  70.2 33.6 %copy-start.9 = (bf16[1,512,2048]{1,2,0:T(8,128)(2,1)S(1)}, bf16[1,512,2048]{1,2,0:T(8,128)(2,1)}, u32[]{:S(2)}) copy-start(bf16[1,512,2048]{1,2,0:T(8,128)(2,1)} %copy.90) | copy-start | bytes 6291460
  73.7 24.6 %collective-permute-start.3 = (f32[16,128,128]{2,1,0:T(8,128)S(1)}, f32[16,128,128]{2,1,0:T(8,128)S(1)}, u32[]{:S(2)}, u32[]{:S(2)}) collective-permute-start(f32[16,128,128]{2,1,0:T(8,128)S(1)} %get-tuple-element.33), channel_id=1, source_target_pairs={{0,8},{4,12},{8,16},{12,20},{16,24},{20,28},{1,9},{5,13},{9,17},{1... | collective-permute-start | bytes 3145736 | tf_op jit(solution)/shard_map/ppermute | solution.py:19
  98.2 5.7 %copy-start.17 = (f32[16,128,128]{2,1,0:T(8,128)}, f32[16,128,128]{2,1,0:T(8,128)S(1)}, u32[]{:S(2)}) copy-start(f32[16,128,128]{2,1,0:T(8,128)S(1)} %collective-permute-done.3) | copy-start | bytes 3145732
  99.7 47.9 %collective-permute-start.4 = (f32[16,128,128]{2,1,0:T(8,128)}, f32[16,128,128]{2,1,0:T(8,128)}, u32[]{:S(2)}, u32[]{:S(2)}) collective-permute-start(f32[16,128,128]{2,1,0:T(8,128)} %multiply_add_fusion.2), channel_id=1, source_target_pairs={{0,16},{4,20},{8,24},{12,28},{1,17},{5,21},{9,25},{13,29},{2,18},{... | collective-permute-start | bytes 3145736 | tf_op jit(solution)/shard_map/ppermute | solution.py:19
  103.9 8.4 %copy-start.7 = (bf16[1,512,2048]{1,2,0:T(8,128)(2,1)S(1)}, bf16[1,512,2048]{1,2,0:T(8,128)(2,1)}, u32[]{:S(2)}) copy-start(bf16[1,512,2048]{1,2,0:T(8,128)(2,1)} %copy-done.6) | copy-start | bytes 6291460
  110.2 6.9 %copy-start.2 = (bf16[16,512,512]{2,1,0:T(8,128)(2,1)}, bf16[16,512,512]{2,1,0:T(8,128)(2,1)S(1)}, u32[]{:S(2)}) copy-start(bf16[16,512,512]{2,1,0:T(8,128)(2,1)S(1)} %multiply_convert_fusion) | copy-start | bytes 25165828
  110.2 37.4 %collective-permute-start.1 = (f32[16]{0:T(128)S(1)}, f32[16]{0:T(128)S(1)}, u32[]{:S(2)}, u32[]{:S(2)}) collective-permute-start(f32[16]{0:T(128)S(1)} %get-tuple-element.30), channel_id=1, source_target_pairs={{0,8},{4,12},{8,16},{12,20},{16,24},{20,28},{1,9},{5,13},{9,17},{1... | collective-permute-start | bytes 200 | tf_op jit(solution)/shard_map/ppermute | solution.py:19
  117.1 32.7 %copy-start.14 = (f32[16,512,128]{1,2,0:T(8,128)S(1)}, f32[16,512,128]{1,2,0:T(8,128)}, u32[]{:S(2)}) copy-start(f32[16,512,128]{1,2,0:T(8,128)} %fusion.30) | copy-start | bytes 12582916
  149.8 2.3 copy-start.21
  160.2 12.2 %copy-start.5 = (bf16[1,512,2048]{1,2,0:T(8,128)(2,1)S(1)}, bf16[1,512,2048]{1,2,0:T(8,128)(2,1)}, u32[]{:S(2)}) copy-start(bf16[1,512,2048]{1,2,0:T(8,128)(2,1)} %copy.91) | copy-start | bytes 6291460
  168.2 4.3 %copy-start.3 = (bf16[16,512,512]{2,1,0:T(8,128)(2,1)}, bf16[16,512,512]{2,1,0:T(8,128)(2,1)S(1)}, u32[]{:S(2)}) copy-start(bf16[16,512,512]{2,1,0:T(8,128)(2,1)S(1)} %multiply_convert_fusion.1) | copy-start | bytes 25165828
  168.2 30.6 %slice-start = ((s8[8388608]{0:T(1024)(128)(4,1)}), s8[4194304]{0:T(1024)(128)(4,1)S(1)}, s32[]{:S(2)}) async-start(s8[8388608]{0:T(1024)(128)(4,1)} %bitcast.105), calls=%async_computation.2 | async-start | bytes 8388608
  168.2 7.7 %copy-start.10 = (bf16[1,512,2048]{1,2,0:T(8,128)(2,1)S(1)}, bf16[1,512,2048]{1,2,0:T(8,128)(2,1)}, u32[]{:S(2)}) copy-start(bf16[1,512,2048]{1,2,0:T(8,128)(2,1)} %copy.90) | copy-start | bytes 6291460
  168.2 30.6 %slice-start.1 = ((s8[8388608]{0:T(1024)(128)(4,1)}), s8[4194304]{0:T(1024)(128)(4,1)S(1)}, s32[]{:S(2)}) async-start(s8[8388608]{0:T(1024)(128)(4,1)} %bitcast.105), calls=%async_computation.3 | async-start | bytes 8388608
  168.2 26.1 %collective-permute-start.8 = (f32[16,128,128]{2,1,0:T(8,128)}, f32[16,128,128]{2,1,0:T(8,128)}, u32[]{:S(2)}, u32[]{:S(2)}) collective-permute-start(f32[16,128,128]{2,1,0:T(8,128)} %get-tuple-element.32), channel_id=1, source_target_pairs={{8,0},{12,4},{16,8},{20,12},{24,16},{28,20},{9,1},{13,5},{17,9},{2... | collective-permute-start | bytes 3145736 | tf_op jit(solution)/shard_map/ppermute | solution.py:19
  184.1 18.0 %collective-permute-start.6 = (f32[16]{0:T(128)S(1)}, f32[16]{0:T(128)S(1)}, u32[]{:S(2)}, u32[]{:S(2)}) collective-permute-start(f32[16]{0:T(128)S(1)} %get-tuple-element.19), channel_id=1, source_target_pairs={{8,0},{12,4},{16,8},{20,12},{24,16},{28,20},{9,1},{13,5},{17,9},{2... | collective-permute-start | bytes 200 | tf_op jit(solution)/shard_map/ppermute | solution.py:19
  197.0 5.1 %copy-start.13 = (f32[16,512,128]{1,2,0:T(8,128)S(1)}, f32[16,512,128]{1,2,0:T(8,128)}, u32[]{:S(2)}) copy-start(f32[16,512,128]{1,2,0:T(8,128)} %fusion.28) | copy-start | bytes 12582916
  197.0 25.7 %collective-permute-start.9 = (f32[16,128,128]{2,1,0:T(8,128)}, f32[16,128,128]{2,1,0:T(8,128)}, u32[]{:S(2)}, u32[]{:S(2)}) collective-permute-start(f32[16,128,128]{2,1,0:T(8,128)} %multiply_add_fusion), channel_id=1, source_target_pairs={{16,0},{20,4},{24,8},{28,12},{17,1},{21,5},{25,9},{29,13},{18,2},{... | collective-permute-start | bytes 3145736 | tf_op jit(solution)/shard_map/ppermute | solution.py:19
  205.6 19.3 %copy-start.8 = (bf16[1,512,2048]{1,2,0:T(8,128)(2,1)S(1)}, bf16[1,512,2048]{1,2,0:T(8,128)(2,1)}, u32[]{:S(2)}) copy-start(bf16[1,512,2048]{1,2,0:T(8,128)(2,1)} %copy-done.6) | copy-start | bytes 6291460
  209.7 15.2 %copy-start.12 = (f32[16,512,128]{1,2,0:T(8,128)S(1)}, f32[16,512,128]{1,2,0:T(8,128)}, u32[]{:S(2)}) copy-start(f32[16,512,128]{1,2,0:T(8,128)} %fusion.31) | copy-start | bytes 12582916
  228.2 4.1 %copy-start.11 = (bf16[1,512,2048]{1,2,0:T(8,128)(2,1)S(1)}, bf16[1,512,2048]{1,2,0:T(8,128)(2,1)}, u32[]{:S(2)}) copy-start(bf16[1,512,2048]{1,2,0:T(8,128)(2,1)} %copy.90) | copy-start | bytes 6291460
  232.3 150.7 %copy-start.1 = (f32[1,512,16]{1,2,0:T(8,128)S(1)}, f32[1,512,16]{1,2,0:T(8,128)}, u32[]{:S(2)}) copy-start(f32[1,512,16]{1,2,0:T(8,128)} %param.13) | copy-start | bytes 98308
Sparse Core Ops, SparseCore 0:
  160.4 222.5 reduce-scatter.1
